TPU v7x, 32 devices: a whole 2x2x4 slice. The times are simulated.
32 devices in a mesh: dp: 8 (over y, x, core), expert: 4 (over z).
Axes of the slice: x: 2, y: 2, z: 4, core: 2. Of those that a mesh axis runs over, the one named last changes fastest.
Arguments:
- hidden: bfloat16 [2, 512, 2880], P(None, ('dp', 'expert')), may hold values from -1.5 to 1.5
- norm_gain: float32 [2880], replicated, may hold values from 0.1 to 1.9
- router: bfloat16 [2880, 64], replicated, may hold values from -0.078125 to 0.078125
- routes: int32 [2, 512, 4], P(None, ('dp', 'expert')), may hold values from 0 to 63, all different within a row; in each aligned block of 16 rows (0 to 15, 16 to 31, ..., all dimensions but the last counted through in order) at most 2 rows name the same one
- w_gate: bfloat16 [64, 2880, 2048], P('expert', None, 'dp'), may hold values from -0.109375 to 0.109375
- w_up: bfloat16 [64, 2880, 2048], P('expert', None, 'dp'), may hold values from -0.109375 to 0.109375
- w_down: bfloat16 [64, 2048, 2880], P('expert', 'dp'), may hold values from -0.125 to 0.125
- queries: bfloat16 [2, 512, 4096], P(None, ('dp', 'expert')), may hold values from -5.5 to 5.5
- new_key: bfloat16 [2, 512, 512], P(None, ('dp', 'expert')), may hold values from -8 to 8
- new_value: bfloat16 [2, 512, 512], P(None, ('dp', 'expert')), may hold values from -6 to 6
- key_pages: bfloat16 [256, 4, 16, 512], P(('dp', 'expert')), may hold values from -6 to 6
- value_pages: bfloat16 [256, 4, 16, 512], P(('dp', 'expert')), may hold values from -6 to 6
- page_counts: int32 [32, 16], P(('dp', 'expert')), may hold values from 1 to 10, 32 in all within a row
- page_order: int32 [32, 32], P(('dp', 'expert')), may hold values from 0 to 31, each once within a row
Outputs:
- context: bfloat16 [2, 512, 4096], P(None, ('dp', 'expert'))
- layer_out: bfloat16 [2, 512, 2880], P(None, ('dp', 'expert'))
Inputs may be any that keep to these rules, and one draw needn't show every extreme that they name: `routes`: in each step, the 16 rows of one aligned block name each expert at most 2 times, and some block names some expert exactly 2 times. `page_counts`: each block's counts sum to 32, and the largest count of a block is exactly 10. Each row of page_order is a permutation of 0 to 31.
All inputs are finite; a program needn't handle non-finite values.
Results may differ from a plain program's by a relative error of at most 0.0095.
Values may be sent and summed in bfloat16 or wider, within the bound.
No kernel may reach another device: no remote copies, remote signals or barrier semaphores. Data moves between devices by JAX's collectives and lax.ppermute only.
A program may use at most 192 MiB of HBM per device.

v0:
```python
import jax
import jax.numpy as jnp
from jax import lax
from jax.sharding import PartitionSpec as P

HEADS = 64
KV_HEADS = 8
HEAD_DIM = 64
EXPERTS = 64
MOST = 2
STEPS = 2
BLOCK = 16


def page_layout(counts, page_perm, most_pages):
    starts = jnp.cumsum(counts) - counts
    offsets = jnp.arange(most_pages, dtype=jnp.int32)
    places = starts[:, None] + offsets[None, :]
    places = jnp.where(offsets[None, :] < counts[:, None], places, 0)
    return jnp.take(page_perm, places, axis=0)


def attention(query_rows, fresh_keys, fresh_values, space_keys, space_values, counts, page_perm):
    group_size = HEADS // KV_HEADS
    most_pages = page_perm.shape[0] // 3
    row_count = counts.shape[0]
    cache_span = most_pages * BLOCK
    slot_ids = page_layout(counts, page_perm, most_pages).reshape(-1)
    cache_keys = jnp.take(space_keys, slot_ids, axis=0).reshape(
        row_count, cache_span, KV_HEADS, HEAD_DIM
    )
    cache_values = jnp.take(space_values, slot_ids, axis=0).reshape(
        row_count, cache_span, KV_HEADS, HEAD_DIM
    )
    live_mask = jnp.arange(cache_span)[None, :] < (counts * BLOCK)[:, None]
    query_heads = query_rows.reshape(STEPS, row_count, KV_HEADS, group_size, HEAD_DIM)
    new_keys = fresh_keys.reshape(STEPS, row_count, KV_HEADS, HEAD_DIM)
    new_values = fresh_values.reshape(STEPS, row_count, KV_HEADS, HEAD_DIM)
    score_scale = HEAD_DIM ** (-0.5)
    old_scores = (
        jnp.einsum("trkgh,rlkh->trkgl", query_heads, cache_keys, preferred_element_type=jnp.float32)
        * score_scale
    )
    old_scores = jnp.where(live_mask[None, :, None, None, :], old_scores, -jnp.inf)
    new_scores = (
        jnp.einsum("trkgh,urkh->trkgu", query_heads, new_keys, preferred_element_type=jnp.float32)
        * score_scale
    )
    causal = jnp.arange(STEPS)[None, :] <= jnp.arange(STEPS)[:, None]
    new_scores = jnp.where(causal[:, None, None, None, :], new_scores, -jnp.inf)
    row_max = jnp.maximum(jnp.max(old_scores, axis=-1), jnp.max(new_scores, axis=-1))
    old_probs = jnp.exp(old_scores - row_max[..., None])
    new_probs = jnp.exp(new_scores - row_max[..., None])
    denominator = jnp.sum(old_probs, axis=-1) + jnp.sum(new_probs, axis=-1)
    numerator = jnp.einsum(
        "trkgl,rlkh->trkgh",
        old_probs.astype(jnp.bfloat16),
        cache_values,
        preferred_element_type=jnp.float32,
    )
    numerator = numerator + jnp.einsum(
        "trkgu,urkh->trkgh",
        new_probs.astype(jnp.bfloat16),
        new_values,
        preferred_element_type=jnp.float32,
    )
    result = numerator / denominator[..., None]
    return result.reshape(STEPS, row_count, HEADS * HEAD_DIM).astype(jnp.bfloat16)


MOST = 2


def moe_layer(hidden, norm_gain, router, routes, w_gate, w_up, w_down):
    steps, rows, model_width = hidden.shape
    topk = routes.shape[-1]
    n_dp = lax.axis_size("dp")
    n_ex = lax.axis_size("expert")
    local_experts = w_gate.shape[0]
    blocks = n_dp * n_ex
    residual = hidden.astype(jnp.float32)
    scale_rows = lax.rsqrt(jnp.mean(residual * residual, axis=-1, keepdims=True) + 1e-05)
    normed = (residual * scale_rows * norm_gain).astype(jnp.bfloat16)
    logit_rows = jnp.einsum("trd,de->tre", normed, router, preferred_element_type=jnp.float32)
    chosen = jnp.take_along_axis(logit_rows, routes, axis=-1)
    spreads = chosen[..., None, :] - chosen[..., :, None]
    gate_vals = (1.0 / jnp.sum(jnp.exp(spreads), axis=-1)).astype(jnp.bfloat16)
    lanes = -(-(model_width + 2 * topk) // 128) * 128
    filler = jnp.zeros((steps, rows, lanes - model_width - 2 * topk), jnp.bfloat16)
    payload = jnp.concatenate([normed, gate_vals, routes.astype(jnp.bfloat16), filler], axis=-1)
    gathered = lax.all_gather(payload, ("dp", "expert"), axis=1, tiled=False)
    return (gathered, residual)


def moe_finish(gathered, meta, residual, topk, w_gate, w_up, w_down):
    steps, rows, model_width = residual.shape
    n_dp = lax.axis_size("dp")
    n_ex = lax.axis_size("expert")
    local_experts = w_gate.shape[0]
    all_rows = gathered[..., :model_width]
    all_gates = meta[..., :topk]
    all_ids = jnp.round(meta[..., topk : 2 * topk]).astype(jnp.int32)
    first = lax.axis_index("expert") * local_experts
    numbers = first + jnp.arange(local_experts, dtype=jnp.int32)
    matches = all_ids[..., None] == numbers
    picked = jnp.any(matches, axis=-2).astype(jnp.int32)
    gate_of = jnp.sum(jnp.where(matches, all_gates[..., None].astype(jnp.float32), 0.0), axis=-2)
    earlier = jnp.cumsum(picked, axis=2) - picked
    ranks = jnp.arange(MOST, dtype=jnp.int32)
    sender = (picked[..., None] > 0) & (earlier[..., None] == ranks)
    slots = jnp.einsum(
        "tbrxm,tbrd->tbxmd",
        sender.astype(jnp.bfloat16),
        all_rows,
        preferred_element_type=jnp.float32,
    ).astype(jnp.bfloat16)
    gate_part = jnp.einsum("tbxmd,xdf->tbxmf", slots, w_gate, preferred_element_type=jnp.float32)
    up_part = jnp.einsum("tbxmd,xdf->tbxmf", slots, w_up, preferred_element_type=jnp.float32)
    hidden_act = ((up_part + 1.0) * gate_part * jax.nn.sigmoid(1.702 * gate_part)).astype(
        jnp.bfloat16
    )
    partial = jnp.einsum(
        "tbxmf,xfd->tbxmd", hidden_act, w_down, preferred_element_type=jnp.float32
    ).astype(jnp.bfloat16)
    weights = jnp.where(sender, gate_of[..., None], 0.0).astype(jnp.bfloat16)
    grid = (steps, n_dp, n_ex)
    if local_experts * MOST < rows:
        summed = lax.psum_scatter(
            partial.astype(jnp.float32).reshape(grid + partial.shape[2:]),
            "dp",
            scatter_dimension=1,
            tiled=True,
        )[:, 0]
        own = lax.axis_index("dp")
        own_weights = lax.dynamic_index_in_dim(
            weights.reshape(grid + weights.shape[2:]), own, 1, False
        )
        row_terms = jnp.einsum(
            "terxm,texmd->terd",
            own_weights.astype(jnp.float32),
            summed,
            precision=lax.Precision.HIGHEST,
            preferred_element_type=jnp.float32,
        )
    else:
        row_terms = jnp.einsum(
            "tbrxm,tbxmd->btrd", weights, partial, preferred_element_type=jnp.float32
        ).astype(jnp.bfloat16)
        row_terms = lax.psum_scatter(
            row_terms.reshape((n_dp, n_ex) + row_terms.shape[1:]),
            "dp",
            scatter_dimension=0,
            tiled=True,
        )[0]
        shares = lax.all_to_all(row_terms, "expert", split_axis=0, concat_axis=0, tiled=True)
        branch_out = jnp.sum(shares.astype(jnp.float32), axis=0)
        return (residual + branch_out).astype(jnp.bfloat16)
    branch_out = lax.psum_scatter(row_terms, "expert", scatter_dimension=1, tiled=True)
    return (residual + branch_out[:, 0].astype(jnp.float32)).astype(jnp.bfloat16)


def body(
    hidden,
    norm_gain,
    router,
    routes,
    w_gate,
    w_up,
    w_down,
    queries,
    new_key,
    new_value,
    key_pages,
    value_pages,
    page_counts,
    page_order,
):
    host_keys, host_values = (
        lax.all_to_all(key_pages, "dp", split_axis=0, concat_axis=0, tiled=True),
        lax.all_to_all(value_pages, "dp", split_axis=0, concat_axis=0, tiled=True),
    )
    kv_width = KV_HEADS * HEAD_DIM
    space_keys = host_keys.reshape(-1, BLOCK, kv_width)
    space_values = host_values.reshape(-1, BLOCK, kv_width)
    gathered, residual = moe_layer(hidden, norm_gain, router, routes, w_gate, w_up, w_down)
    context = attention(
        queries, new_key, new_value, space_keys, space_values, page_counts[0], page_order[0]
    )
    meta = gathered[..., hidden.shape[-1] :]
    gathered, meta, context = lax.optimization_barrier((gathered, meta, context))
    layer_out = moe_finish(gathered, meta, residual, routes.shape[-1], w_gate, w_up, w_down)
    return (context, layer_out)


def solution(mesh):
    return jax.shard_map(
        body,
        mesh=mesh,
        in_specs=(
            P(None, ("dp", "expert"), None),
            P(),
            P(),
            P(None, ("dp", "expert"), None),
            P("expert", None, "dp"),
            P("expert", None, "dp"),
            P("expert", "dp", None),
            P(None, ("dp", "expert"), None),
            P(None, ("dp", "expert"), None),
            P(None, ("dp", "expert"), None),
            P(("dp", "expert"), None, None, None),
            P(("dp", "expert"), None, None, None),
            P(("dp", "expert"), None),
            P(("dp", "expert"), None),
        ),
        out_specs=(P(None, ("dp", "expert"), None), P(None, ("dp", "expert"), None)),
        check_vma=False,
    )
```

profile of v0, /device:TPU:0, one launch (start us, length us, event | category | flops | bytes accessed | tf_op | source)
XLA Modules:
  0.0 261.9 jit_solution(6205403180816961716)
XLA Ops:
  11.5 1.5 gather_fusion.1
  14.2 5.2 %all-to-all-start = ((bf16[8,4,16,512]{3,2,1,0:T(8,128)(2,1)}), bf16[8,4,16,512]{3,2,1,0:T(8,128)(2,1)S(1)}, u32[]{:S(2)}, u32[]{:S(2)}) async-start(bf16[8,4,16,512]{3,2,1,0:T(8,128)(2,1)} %param.27), calls=%async_computation | async-start | bytes 1048576 | tf_op jit(solution)/shard_map/all_to_all | solution.py:180
  21.1 1.6 gather_fusion
  22.7 6.6 %all-to-all-done = bf16[8,4,16,512]{3,2,1,0:T(8,128)(2,1)S(1)} async-done(((bf16[8,4,16,512]{3,2,1,0:T(8,128)(2,1)}), bf16[8,4,16,512]{3,2,1,0:T(8,128)(2,1)S(1)}, u32[]{:S(2)}, u32[]{:S(2)}) %all-to-all-start) | async-done | bytes 524320 | tf_op jit(solution)/shard_map/all_to_all | solution.py:180
  29.3 3.5 %all-to-all-start.1 = ((bf16[8,4,16,512]{3,2,1,0:T(8,128)(2,1)}), bf16[8,4,16,512]{3,2,1,0:T(8,128)(2,1)S(1)}, u32[]{:S(2)}, u32[]{:S(2)}) async-start(bf16[8,4,16,512]{3,2,1,0:T(8,128)(2,1)} %param.26), calls=%async_computation.1 | async-start | bytes 1048576 | tf_op jit(solution)/shard_map/all_to_all | solution.py:179
  32.9 3.2 %fusion.68 = (f32[2,16,8,8]{3,0,2,1:T(2,128)S(1)}, f32[2,16,8,8,2]{3,4,0,2,1:T(2,128)}) fusion(bf16[2,16,8,8,64]{4,3,2,1,0:T(8,128)(2,1)S(1)} %reshape.268, bf16[2,16,8,64,1]{3,2,1,0,4:T(8,128)(2,1)S(1)} %bitcast.102, pred[2,2]{1,0:T(4,128)(4,1)S(1)} %iota_compare_fusion.3), kind=kOutput, calls=%fused_computation.101 | convolution fusion | flops 534528 | bytes 319492 | tf_op jit(solution)/shard_map/trkgh,urkh->trkgu/dot_general | solution.py:46
  36.1 2.5 gather_fusion.2
  38.6 3.9 %all-to-all-done.1 = bf16[8,4,16,512]{3,2,1,0:T(8,128)(2,1)S(1)} async-done(((bf16[8,4,16,512]{3,2,1,0:T(8,128)(2,1)}), bf16[8,4,16,512]{3,2,1,0:T(8,128)(2,1)S(1)}, u32[]{:S(2)}, u32[]{:S(2)}) %all-to-all-start.1) | async-done | bytes 524320 | tf_op jit(solution)/shard_map/all_to_all | solution.py:179
  42.4 2.5 gather_fusion.3
  44.9 4.4 %broadcast_select_fusion = (bf16[160,16,512]{2,1,0:T(8,128)(2,1)}, bf16[160,16,512]{2,1,0:T(8,128)(2,1)S(1)}) fusion(bf16[160,16,512]{2,1,0:T(8,128)(2,1)} %gather_fusion.3, pred[160]{0:T(512)(128)(4,1)S(1)} %get-tuple-element.9, bf16[160,16,512]{2,1,0:T(8,128)(2,1)} %gather_fusion.2), kind=kLoop, calls=%fused_computation.23 | loop fusion | flops 2621440 | bytes 10485920 | tf_op jit(solution)/shard_map/jit(_take)/select_n | solution.py:29
  49.4 7.5 %reshape.267 = bf16[16,160,8,64]{3,2,1,0:T(8,128)(2,1)} reshape(bf16[160,16,512]{2,1,0:T(8,128)(2,1)} %get-tuple-element.15) | data formatting | bytes 5242880 | tf_op jit(solution)/shard_map/reshape | solution.py:29
  56.8 4.6 %reshape.265 = bf16[16,160,8,64]{3,2,1,0:T(8,128)(2,1)} reshape(bf16[160,16,512]{2,1,0:T(8,128)(2,1)S(1)} %get-tuple-element.16) | data formatting | bytes 5242880 | tf_op jit(solution)/shard_map/reshape | solution.py:32
  61.4 6.4 %bitcast_reduce_fusion = (f32[2,16,8,8]{3,0,2,1:T(2,128)S(1)}, f32[16,8,160,2,8]{2,4,3,1,0:T(8,128)S(1)}) fusion(pred[16,160]{1,0:T(8,128)(4,1)S(1)} %iota_compare_fusion.1, bf16[2,16,8,8,64]{4,3,2,1,0:T(8,128)(2,1)S(1)} %reshape.268, bf16[16,160,8,64,1]{3,2,1,0,4:T(8,128)(2,1)} %bitcast.99), kind=kOutput, calls=%fused_computation.26 | convolution fusion | flops 42924032 | bytes 4205056 | tf_op jit(solution)/shard_map/trkgh,rlkh->trkgl/dot_general | solution.py:41
  69.5 1.5 fusion.27
  71.8 1.2 convert_element_type.77
  73.0 12.4 %all-gather.3.cloned.1.call-done = bf16[2,512,2944]{2,1,0:T(8,128)(2,1)} async-done(((bf16[2,16,2944]{2,1,0:T(8,128)(2,1)}), bf16[2,512,2944]{2,1,0:T(8,128)(2,1)}) %all-gather.3.cloned.1.call-update) | async-done | bytes 6029328 | tf_op jit(solution)/shard_map/all_gather | solution.py:91
  85.4 1.1 slice.25
  88.9 10.5 %convolution_convert_fusion = bf16[2,32,16,2,2880]{4,2,3,1,0:T(8,128)(2,1)} fusion(bf16[2,32,16,2944]{3,2,1,0:T(8,128)(2,1)} %bitcast.93, s32[2,32,16,16]{3,2,0,1:T(8,128)S(1)} %copy.125, pred[2,32,16,16]{3,2,0,1:T(8,128)(4,1)S(1)} %copy.124), kind=kOutput, calls=%fused_computation.16 | convolution fusion | flops 194707456 | bytes 17907712 | tf_op jit(solution)/shard_map/tbrxm,tbrd->tbxmd/dot_general | solution.py:111
  99.4 13.9 %fusion.4 = f32[16,2,32,2,256]{4,2,3,1,0:T(8,128)S(1)} fusion(bf16[16,2880,256]{2,1,0:T(8,128)(2,1)} %param.21, bf16[2,32,16,2,2880]{4,2,3,1,0:T(8,128)(2,1)} %convolution_convert_fusion), kind=kOutput, calls=%fused_computation.8 | convolution fusion | flops 3019898880 | bytes 37486592 | tf_op jit(solution)/shard_map/tbxmd,xdf->tbxmf/dot_general | solution.py:118
  113.3 13.9 %fusion.32 = bf16[2,32,16,2,256]{4,1,3,0,2:T(8,128)(2,1)S(1)} fusion(bf16[16,2880,256]{2,1,0:T(8,128)(2,1)} %param.20, bf16[2,32,16,2,2880]{4,2,3,1,0:T(8,128)(2,1)} %convolution_convert_fusion, f32[16,2,32,2,256]{4,2,3,1,0:T(8,128)S(1)} %fusion.4), kind=kOutput, calls=%fused_computation.37 | convolution fusion | flops 3024093184 | bytes 38535168 | tf_op jit(solution)/shard_map/tbxmd,xdf->tbxmf/dot_general | solution.py:117
  127.3 23.1 %convert_bitcast_fusion = bf16[2,32,16,2,2880]{4,1,3,0,2:T(8,128)(2,1)} fusion(bf16[2,32,16,2,256]{4,1,3,0,2:T(8,128)(2,1)S(1)} %fusion.32, bf16[16,256,2880]{1,2,0:T(8,128)(2,1)} %param.22), kind=kOutput, calls=%fused_computation.13 | convolution fusion | flops 3025797120 | bytes 36438016 | tf_op jit(solution)/shard_map/tbxmf,xfd->tbxmd/dot_general | solution.py:122
  150.4 20.2 %bitcast_convert_fusion = bf16[32,2,16,2880]{3,2,1,0:T(8,128)(2,1)} fusion(bf16[2,32,16,2,2880]{4,1,3,0,2:T(8,128)(2,1)} %convert_bitcast_fusion, bf16[2,32,16,16]{3,2,0,1:T(8,128)(2,1)S(1)} %copy.127, s32[2,32,16,16]{3,2,0,1:T(8,128)S(1)} %copy.125, pred[2,32,16,16]{3,2,0,1:T(8,128)(4,1)S(1)} %copy.124), kind=kOutput, calls=%fused_computation.10 | convolution fusion | flops 191791104 | bytes 17809408 | tf_op jit(solution)/shard_map/tbrxm,tbxmd->btrd/dot_general | solution.py:146
  170.6 59.4 %reduce-scatter.2.cloned.1.call-done = bf16[1,4,2,16,2880]{4,3,2,1,0:T(8,128)(2,1)} async-done(((bf16[8,4,2,16,2880]{4,3,2,1,0:T(8,128)(2,1)}), bf16[1,4,2,16,2880]{4,3,2,1,0:T(8,128)(2,1)}) %reduce-scatter.2.cloned.1.call-update) | async-done | bytes 737296 | tf_op jit(solution)/shard_map/reduce_scatter | solution.py:149
  230.0 24.0 %all_to_all.15 = bf16[4,2,16,2880]{3,2,1,0:T(8,128)(2,1)S(1)} all-to-all(bf16[4,2,16,2880]{3,2,1,0:T(8,128)(2,1)} %bitcast.100), channel_id=1, replica_groups=mesh['dp'=8,'expert'=4] {'expert'}, dimensions={0} | all-to-all | bytes 1474560 | tf_op jit(solution)/shard_map/all_to_all | solution.py:155
  (88 shorter events, 12.8 us)
Async XLA Ops:
  7.2 4.1 %copy-start = (bf16[2880,64]{0,1:T(8,128)(2,1)S(1)}, bf16[2880,64]{0,1:T(8,128)(2,1)}, u32[]{:S(2)}) copy-start(bf16[2880,64]{0,1:T(8,128)(2,1)} %param.18) | copy-start | bytes 1105924
  7.2 78.2 %all-gather.3.cloned.1.call-start = ((), (), s32[]{:S(2)}) async-start(), calls=%async_computation.5 | async-start | bytes 6217728 | tf_op jit(solution)/shard_map/all_gather | solution.py:91
  11.5 7.9 %copy-start.8 = (s32[1,16]{1,0:T(1,128)S(1)}, s32[1,16]{1,0:T(1,128)}, u32[]{:S(2)}) copy-start(s32[1,16]{1,0:T(1,128)} %param.28) | copy-start | bytes 196
  11.5 8.8 %copy-start.6 = (bf16[2,16,512]{2,1,0:T(8,128)(2,1)S(1)}, bf16[2,16,512]{2,1,0:T(8,128)(2,1)}, u32[]{:S(2)}) copy-start(bf16[2,16,512]{2,1,0:T(8,128)(2,1)} %param.24) | copy-start | bytes 98308
  11.5 8.9 %copy-start.7 = (bf16[2,16,512]{2,1,0:T(8,128)(2,1)S(1)}, bf16[2,16,512]{2,1,0:T(8,128)(2,1)}, u32[]{:S(2)}) copy-start(bf16[2,16,512]{2,1,0:T(8,128)(2,1)} %param.25) | copy-start | bytes 98308
  11.5 9.0 %copy-start.4 = (bf16[2,16,4096]{2,1,0:T(8,128)(2,1)S(1)}, bf16[2,16,4096]{2,1,0:T(8,128)(2,1)}, u32[]{:S(2)}) copy-start(bf16[2,16,4096]{2,1,0:T(8,128)(2,1)} %param.23) | copy-start | bytes 786436
  13.1 8.0 %copy-start.2 = (s32[1,32]{1,0:T(1,128)S(1)}, s32[1,32]{1,0:T(1,128)}, u32[]{:S(2)}) copy-start(s32[1,32]{1,0:T(1,128)} %param.29) | copy-start | bytes 388
  14.2 15.0 %all-to-all-start = ((bf16[8,4,16,512]{3,2,1,0:T(8,128)(2,1)}), bf16[8,4,16,512]{3,2,1,0:T(8,128)(2,1)S(1)}, u32[]{:S(2)}, u32[]{:S(2)}) async-start(bf16[8,4,16,512]{3,2,1,0:T(8,128)(2,1)} %param.27), calls=%async_computation | async-start | bytes 1048576 | tf_op jit(solution)/shard_map/all_to_all | solution.py:180
  29.3 13.2 %all-to-all-start.1 = ((bf16[8,4,16,512]{3,2,1,0:T(8,128)(2,1)}), bf16[8,4,16,512]{3,2,1,0:T(8,128)(2,1)S(1)}, u32[]{:S(2)}, u32[]{:S(2)}) async-start(bf16[8,4,16,512]{3,2,1,0:T(8,128)(2,1)} %param.26), calls=%async_computation.1 | async-start | bytes 1048576 | tf_op jit(solution)/shard_map/all_to_all | solution.py:179
  32.8 197.2 %reduce-scatter.2.cloned.1.call-start = ((), (), s32[]{:S(2)}) async-start(), calls=%async_computation.4 | async-start | bytes 6782976 | tf_op jit(solution)/shard_map/reduce_scatter | solution.py:149
  61.4 8.1 %slice-start = ((s8[5242880]{0:T(1024)(128)(4,1)}), s8[4194304]{0:T(1024)(128)(4,1)S(1)}, s32[]{:S(2)}) async-start(s8[5242880]{0:T(1024)(128)(4,1)} %bitcast.96), calls=%async_computation.6 | async-start | bytes 8388608
  61.4 6.4 %copy-start.5 = (f32[2,16,8,8,2]{3,4,0,2,1:T(2,128)S(1)}, f32[2,16,8,8,2]{3,4,0,2,1:T(2,128)}, u32[]{:S(2)}) copy-start(f32[2,16,8,8,2]{3,4,0,2,1:T(2,128)} %get-tuple-element.20) | copy-start | bytes 49156
  61.4 8.1 %slice-start.1 = ((s8[5242880]{0:T(1024)(128)(4,1)}), s8[1048576]{0:T(1024)(128)(4,1)S(1)}, s32[]{:S(2)}) async-start(s8[5242880]{0:T(1024)(128)(4,1)} %bitcast.96), calls=%async_computation.7 | async-start | bytes 2097152
  170.5 83.6 %copy-start.3 = (bf16[2,16,2880]{2,1,0:T(8,128)(2,1)S(1)}, bf16[2,16,2880]{2,1,0:T(8,128)(2,1)}, u32[]{:S(2)}) copy-start(bf16[2,16,2880]{2,1,0:T(8,128)(2,1)} %param.16) | copy-start | bytes 552964
  170.6 84.3 %copy-start.1 = (bf16[2880,64]{0,1:T(8,128)(2,1)S(1)}, bf16[2880,64]{0,1:T(8,128)(2,1)}, u32[]{:S(2)}) copy-start(bf16[2880,64]{0,1:T(8,128)(2,1)} %param.18) | copy-start | bytes 1105924
Sparse Core Ops, SparseCore 0:
  14.4 70.9 all-gather.2
  170.7 59.2 reduce-scatter.1
where the time goes:
time: 267 us; the launch traced here: 262 us
  matrix products  93.5 us (35%)
  waiting for transfers between devices  82.2 us (31%)
  local copies, waits for them, and re-layouts  27.8 us (10%)
  blocking collectives  24 us (9%)
  between operations  14.7 us (6%)
  other arithmetic  10.8 us (4%)
  starting transfers between devices  8.76 us (3%)
    reduce_scatter x1, waiting for transfers between devices, moe_finish(): lax.psum_scatter(row_terms.reshape((n_dp, n_ex) + row_terms.shape[1:]), '...  59.4 us
    all_to_all x1, blocking collectives, moe_finish(): lax.all_to_all(row_terms, 'expert', split_axis=0, concat_axis=0, tiled=True)  24 us
    dot_general x1, matrix products, moe_finish(): jnp.einsum('tbxmf,xfd->tbxmd', hidden_act, w_down, preferred_element_type...  23.1 us
    dot_general x1, matrix products, moe_finish(): jnp.einsum('tbrxm,tbxmd->btrd', weights, partial, preferred_element_type=...  20.2 us
    dot_general x1, matrix products, moe_finish(): jnp.einsum('tbxmd,xdf->tbxmf', slots, w_gate, preferred_element_type=jnp....  13.9 us
    dot_general x1, matrix products, moe_finish(): jnp.einsum('tbxmd,xdf->tbxmf', slots, w_up, preferred_element_type=jnp.fl...  13.9 us
    all_gather x1, waiting for transfers between devices, moe_layer(): gathered = lax.all_gather(payload, ('dp', 'expert'), axis=1, tiled=False)  12.4 us
    dot_general x1, matrix products, moe_finish(): jnp.einsum('tbrxm,tbrd->tbxmd', sender.astype(jnp.bfloat16), all_rows, pr...  10.5 us
  transfers between devices with their start and end apart: 4, of which 4 were waited for; matrix products, arithmetic and copies ran while one was open for 15% of the time, Pallas kernels for 0%

commit v1 on v0

--- a/solution.py
+++ b/solution.py
@@ -1,3 +1,4 @@
+import functools
 import jax
 import jax.numpy as jnp
 from jax import lax
@@ -10,6 +11,31 @@
 MOST = 2
 STEPS = 2
 BLOCK = 16
+
+
+def launch_sources_all_all(piece_in, row_dim, on_dim):
+    fresh, p_next = (lax.axis_size("dp"), lax.axis_index("dp"))
+    item_now = piece_in.shape[row_dim] // fresh
+    n_now = list(piece_in.shape)
+    n_now[row_dim] = item_now
+    u_next = n_now[on_dim]
+    n_now[on_dim] = u_next * fresh
+    reached = jnp.zeros(n_now, piece_in.dtype)
+    dd = 0
+    while dd < fresh:
+        taken_in = lax.dynamic_slice_in_dim(
+            piece_in, (p_next ^ dd) * item_now, item_now, axis=row_dim
+        )
+        if dd:
+            taken_in = lax.ppermute(taken_in, "dp", [(k, k ^ dd) for k in range(fresh)])
+        reached = lax.dynamic_update_slice_in_dim(
+            reached, taken_in, (p_next ^ dd) * u_next, axis=on_dim
+        )
+        dd = dd + 1
+    return reached
+
+
+process_shards_up = functools.partial(launch_sources_all_all, row_dim=0, on_dim=0)
 
 
 def page_layout(counts, page_perm, most_pages):
@@ -176,7 +202,7 @@
     page_order,
 ):
     host_keys, host_values = (
-        lax.all_to_all(key_pages, "dp", split_axis=0, concat_axis=0, tiled=True),
+        process_shards_up(key_pages),
         lax.all_to_all(value_pages, "dp", split_axis=0, concat_axis=0, tiled=True),
     )
     kv_width = KV_HEADS * HEAD_DIM

time: 267 us -> 268 us (level)
  starting transfers between devices: 8.76 us -> 13.6 us
  waiting for transfers between devices: 82.2 us -> 79 us
    ppermute x0 -> x7, starting transfers between devices: none -> 8.31 us  [launch_sources_all_all(): taken_in = lax.ppermute(taken_in, 'dp', [(k, k ^ dd) for k in range(fresh)])]
    all_to_all x1, waiting for transfers between devices: 6.55 us -> 0.01 us  [body(): lax.all_to_all(value_pages, 'dp', split_axis=0, concat_axis=0, tiled=True)]
    ppermute x0 -> x7, waiting for transfers between devices: none -> 6.41 us  [launch_sources_all_all(): taken_in = lax.ppermute(taken_in, 'dp', [(k, k ^ dd) for k in range(fresh)])]
    all_to_all x1 -> x0, waiting for transfers between devices: 3.87 us -> none  [body(): lax.all_to_all(key_pages, 'dp', split_axis=0, concat_axis=0, tiled=True)]
    all_to_all x1 -> x0, starting transfers between devices: 3.5 us -> none  [body(): lax.all_to_all(key_pages, 'dp', split_axis=0, concat_axis=0, tiled=True)]
  transfers between devices with their start and end apart: 4 -> 10, of which waited for: 4 -> 4; matrix products, arithmetic and copies ran while one was open for 15% -> 15% of each run, Pallas kernels for 0% -> 0%
where the time goes in v1:
time: 268 us; the launch traced here: 265 us
  matrix products  93.5 us (35%)
  waiting for transfers between devices  79 us (29%)
  local copies, waits for them, and re-layouts  29.1 us (11%)
  blocking collectives  24 us (9%)
  between operations  14.9 us (6%)
  starting transfers between devices  13.6 us (5%)
  other arithmetic  10.6 us (4%)
    reduce_scatter x1, waiting for transfers between devices, moe_finish(): lax.psum_scatter(row_terms.reshape((n_dp, n_ex) + row_terms.shape[1:]), '...  59.4 us
    all_to_all x1, blocking collectives, moe_finish(): lax.all_to_all(row_terms, 'expert', split_axis=0, concat_axis=0, tiled=True)  24 us
    dot_general x1, matrix products, moe_finish(): jnp.einsum('tbxmf,xfd->tbxmd', hidden_act, w_down, preferred_element_type...  23.1 us
    dot_general x1, matrix products, moe_finish(): jnp.einsum('tbrxm,tbxmd->btrd', weights, partial, preferred_element_type=...  20.2 us
    dot_general x1, matrix products, moe_finish(): jnp.einsum('tbxmd,xdf->tbxmf', slots, w_gate, preferred_element_type=jnp....  13.9 us
    dot_general x1, matrix products, moe_finish(): jnp.einsum('tbxmd,xdf->tbxmf', slots, w_up, preferred_element_type=jnp.fl...  13.7 us
    all_gather x1, waiting for transfers between devices, moe_layer(): gathered = lax.all_gather(payload, ('dp', 'expert'), axis=1, tiled=False)  13.1 us
    dot_general x1, matrix products, moe_finish(): jnp.einsum('tbrxm,tbrd->tbxmd', sender.astype(jnp.bfloat16), all_rows, pr...  10.5 us
  transfers between devices with their start and end apart: 10, of which 4 were waited for; matrix products, arithmetic and copies ran while one was open for 15% of the time, Pallas kernels for 0%

profile of v1, /device:TPU:0, one launch (start us, length us, event | category | flops | bytes accessed | tf_op | source)
XLA Modules:
  0.0 264.5 jit_solution(14188691641126004756)
XLA Ops:
  11.5 1.5 gather_fusion.1
  14.3 5.2 %all-to-all-start = ((bf16[8,4,16,512]{3,2,1,0:T(8,128)(2,1)}), bf16[8,4,16,512]{3,2,1,0:T(8,128)(2,1)S(1)}, u32[]{:S(2)}, u32[]{:S(2)}) async-start(bf16[8,4,16,512]{3,2,1,0:T(8,128)(2,1)} %param.27), calls=%async_computation | async-start | bytes 1048576 | tf_op jit(solution)/shard_map/all_to_all | solution.py:206
  19.7 2.7 %collective-permute-start.6 = (bf16[1,4,16,512]{3,2,1,0:T(8,128)(2,1)S(1)}, bf16[1,4,16,512]{3,2,1,0:T(8,128)(2,1)S(1)}, u32[]{:S(2)}, u32[]{:S(2)}) collective-permute-start(bf16[1,4,16,512]{3,2,1,0:T(8,128)(2,1)S(1)} %get-tuple-element.13), channel_id=1, source_target_pairs={{0,28},{4,24},{8,20},{12,16},{16,12},{20,8},{24,4},{28,0},{1,29},{... | collective-permute-start | bytes 196616 | tf_op jit(solution)/shard_map/ppermute | solution.py:30
  22.8 1.5 collective-permute-start.3
  27.3 2.0 gather_fusion
  29.4 3.2 %fusion.68 = (f32[2,16,8,8]{3,0,2,1:T(2,128)S(1)}, f32[2,16,8,8,2]{3,4,0,2,1:T(2,128)}) fusion(bf16[2,16,8,8,64]{4,3,2,1,0:T(8,128)(2,1)S(1)} %reshape.268, bf16[2,16,8,64,1]{3,2,1,0,4:T(8,128)(2,1)S(1)} %bitcast.102, pred[2,2]{1,0:T(4,128)(4,1)S(1)} %iota_compare_fusion.3), kind=kOutput, calls=%fused_computation.116 | convolution fusion | flops 534528 | bytes 319492 | tf_op jit(solution)/shard_map/trkgh,urkh->trkgu/dot_general | solution.py:72
  32.6 1.5 collective-permute-start.1
  34.2 2.8 %collective-permute-done.1 = bf16[1,4,16,512]{3,2,1,0:T(8,128)(2,1)S(1)} collective-permute-done((bf16[1,4,16,512]{3,2,1,0:T(8,128)(2,1)S(1)}, bf16[1,4,16,512]{3,2,1,0:T(8,128)(2,1)S(1)}, u32[]{:S(2)}, u32[]{:S(2)}) %collective-permute-start.1) | collective-permute-done | bytes 65568 | tf_op jit(solution)/shard_map/ppermute | solution.py:30
  38.5 3.6 %collective-permute-done.5 = bf16[1,4,16,512]{3,2,1,0:T(8,128)(2,1)S(1)} collective-permute-done((bf16[1,4,16,512]{3,2,1,0:T(8,128)(2,1)S(1)}, bf16[1,4,16,512]{3,2,1,0:T(8,128)(2,1)S(1)}, u32[]{:S(2)}, u32[]{:S(2)}) %collective-permute-start.5) | collective-permute-done | bytes 65568 | tf_op jit(solution)/shard_map/ppermute | solution.py:30
  42.2 2.5 gather_fusion.3
  44.7 2.5 gather_fusion.2
  47.1 4.0 %broadcast_select_fusion = (bf16[160,16,512]{2,1,0:T(8,128)(2,1)}, bf16[160,16,512]{2,1,0:T(8,128)(2,1)S(1)}) fusion(bf16[160,16,512]{2,1,0:T(8,128)(2,1)} %gather_fusion.3, pred[160]{0:T(512)(128)(4,1)S(1)} %get-tuple-element.9, bf16[160,16,512]{2,1,0:T(8,128)(2,1)} %gather_fusion.2), kind=kLoop, calls=%fused_computation.23 | loop fusion | flops 2621440 | bytes 10485920 | tf_op jit(solution)/shard_map/jit(_take)/select_n | solution.py:55
  51.1 7.5 %reshape.267 = bf16[16,160,8,64]{3,2,1,0:T(8,128)(2,1)} reshape(bf16[160,16,512]{2,1,0:T(8,128)(2,1)} %get-tuple-element.23) | data formatting | bytes 5242880 | tf_op jit(solution)/shard_map/reshape | solution.py:55
  58.6 4.6 %reshape.265 = bf16[16,160,8,64]{3,2,1,0:T(8,128)(2,1)} reshape(bf16[160,16,512]{2,1,0:T(8,128)(2,1)S(1)} %get-tuple-element.24) | data formatting | bytes 5242880 | tf_op jit(solution)/shard_map/reshape | solution.py:58
  63.2 6.5 %bitcast_reduce_fusion = (f32[2,16,8,8]{3,0,2,1:T(2,128)S(1)}, f32[16,8,160,2,8]{2,4,3,1,0:T(8,128)S(1)}) fusion(pred[16,160]{1,0:T(8,128)(4,1)S(1)} %iota_compare_fusion.1, bf16[2,16,8,8,64]{4,3,2,1,0:T(8,128)(2,1)S(1)} %reshape.268, bf16[16,160,8,64,1]{3,2,1,0,4:T(8,128)(2,1)} %bitcast.99), kind=kOutput, calls=%fused_computation.26 | convolution fusion | flops 42924032 | bytes 4205056 | tf_op jit(solution)/shard_map/trkgh,rlkh->trkgl/dot_general | solution.py:67
  71.4 1.5 fusion.27
  74.9 13.1 %all-gather.3.cloned.1.call-done = bf16[2,512,2944]{2,1,0:T(8,128)(2,1)} async-done(((bf16[2,16,2944]{2,1,0:T(8,128)(2,1)}), bf16[2,512,2944]{2,1,0:T(8,128)(2,1)}) %all-gather.3.cloned.1.call-update) | async-done | bytes 6029328 | tf_op jit(solution)/shard_map/all_gather | solution.py:117
  91.7 10.5 %convolution_convert_fusion = bf16[2,32,16,2,2880]{4,2,3,1,0:T(8,128)(2,1)} fusion(bf16[2,32,16,2944]{3,2,1,0:T(8,128)(2,1)} %bitcast.93, s32[2,32,16,16]{3,2,0,1:T(8,128)S(1)} %copy.125, pred[2,32,16,16]{3,2,0,1:T(8,128)(4,1)S(1)} %copy.124), kind=kOutput, calls=%fused_computation.16 | convolution fusion | flops 194707456 | bytes 17907712 | tf_op jit(solution)/shard_map/tbrxm,tbrd->tbxmd/dot_general | solution.py:137
  102.3 13.7 %fusion.4 = f32[16,2,32,2,256]{4,2,3,1,0:T(8,128)S(1)} fusion(bf16[16,2880,256]{2,1,0:T(8,128)(2,1)} %param.21, bf16[2,32,16,2,2880]{4,2,3,1,0:T(8,128)(2,1)} %convolution_convert_fusion), kind=kOutput, calls=%fused_computation.8 | convolution fusion | flops 3019898880 | bytes 37486592 | tf_op jit(solution)/shard_map/tbxmd,xdf->tbxmf/dot_general | solution.py:144
  116.0 13.9 %fusion.32 = bf16[2,32,16,2,256]{4,1,3,0,2:T(8,128)(2,1)S(1)} fusion(bf16[16,2880,256]{2,1,0:T(8,128)(2,1)} %param.20, bf16[2,32,16,2,2880]{4,2,3,1,0:T(8,128)(2,1)} %convolution_convert_fusion, f32[16,2,32,2,256]{4,2,3,1,0:T(8,128)S(1)} %fusion.4), kind=kOutput, calls=%fused_computation.37 | convolution fusion | flops 3024093184 | bytes 38535168 | tf_op jit(solution)/shard_map/tbxmd,xdf->tbxmf/dot_general | solution.py:143
  129.9 23.1 %convert_bitcast_fusion = bf16[2,32,16,2,2880]{4,1,3,0,2:T(8,128)(2,1)} fusion(bf16[2,32,16,2,256]{4,1,3,0,2:T(8,128)(2,1)S(1)} %fusion.32, bf16[16,256,2880]{1,2,0:T(8,128)(2,1)} %param.22), kind=kOutput, calls=%fused_computation.13 | convolution fusion | flops 3025797120 | bytes 36438016 | tf_op jit(solution)/shard_map/tbxmf,xfd->tbxmd/dot_general | solution.py:148
  153.0 20.2 %bitcast_convert_fusion = bf16[32,2,16,2880]{3,2,1,0:T(8,128)(2,1)} fusion(bf16[2,32,16,2,2880]{4,1,3,0,2:T(8,128)(2,1)} %convert_bitcast_fusion, bf16[2,32,16,16]{3,2,0,1:T(8,128)(2,1)S(1)} %copy.127, s32[2,32,16,16]{3,2,0,1:T(8,128)S(1)} %copy.125, pred[2,32,16,16]{3,2,0,1:T(8,128)(4,1)S(1)} %copy.124), kind=kOutput, calls=%fused_computation.10 | convolution fusion | flops 191791104 | bytes 17809408 | tf_op jit(solution)/shard_map/tbrxm,tbxmd->btrd/dot_general | solution.py:172
  173.2 59.4 %reduce-scatter.2.cloned.1.call-done = bf16[1,4,2,16,2880]{4,3,2,1,0:T(8,128)(2,1)} async-done(((bf16[8,4,2,16,2880]{4,3,2,1,0:T(8,128)(2,1)}), bf16[1,4,2,16,2880]{4,3,2,1,0:T(8,128)(2,1)}) %reduce-scatter.2.cloned.1.call-update) | async-done | bytes 737296 | tf_op jit(solution)/shard_map/reduce_scatter | solution.py:175
  232.7 24.0 %all_to_all.10 = bf16[4,2,16,2880]{3,2,1,0:T(8,128)(2,1)S(1)} all-to-all(bf16[4,2,16,2880]{3,2,1,0:T(8,128)(2,1)} %bitcast.100), channel_id=1, replica_groups=mesh['dp'=8,'expert'=4] {'expert'}, dimensions={0} | all-to-all | bytes 1474560 | tf_op jit(solution)/shard_map/all_to_all | solution.py:181
  (113 shorter events, 18.7 us)
Async XLA Ops:
  7.2 4.1 %copy-start = (bf16[2880,64]{0,1:T(8,128)(2,1)S(1)}, bf16[2880,64]{0,1:T(8,128)(2,1)}, u32[]{:S(2)}) copy-start(bf16[2880,64]{0,1:T(8,128)(2,1)} %param.18) | copy-start | bytes 1105924
  7.2 80.8 %all-gather.3.cloned.1.call-start = ((), (), s32[]{:S(2)}) async-start(), calls=%async_computation.4 | async-start | bytes 6217728 | tf_op jit(solution)/shard_map/all_gather | solution.py:117
  13.0 6.6 %copy-start.4 = (bf16[8,4,16,512]{3,2,1,0:T(8,128)(2,1)S(1)}, bf16[8,4,16,512]{3,2,1,0:T(8,128)(2,1)}, u32[]{:S(2)}) copy-start(bf16[8,4,16,512]{3,2,1,0:T(8,128)(2,1)} %param.26) | copy-start | bytes 1572868
  13.0 12.0 %copy-start.10 = (s32[1,16]{1,0:T(1,128)S(1)}, s32[1,16]{1,0:T(1,128)}, u32[]{:S(2)}) copy-start(s32[1,16]{1,0:T(1,128)} %param.28) | copy-start | bytes 196
  13.1 12.8 %copy-start.8 = (bf16[2,16,512]{2,1,0:T(8,128)(2,1)S(1)}, bf16[2,16,512]{2,1,0:T(8,128)(2,1)}, u32[]{:S(2)}) copy-start(bf16[2,16,512]{2,1,0:T(8,128)(2,1)} %param.24) | copy-start | bytes 98308
  13.1 12.9 %copy-start.9 = (bf16[2,16,512]{2,1,0:T(8,128)(2,1)S(1)}, bf16[2,16,512]{2,1,0:T(8,128)(2,1)}, u32[]{:S(2)}) copy-start(bf16[2,16,512]{2,1,0:T(8,128)(2,1)} %param.25) | copy-start | bytes 98308
  13.1 13.6 %copy-start.5 = (bf16[2,16,4096]{2,1,0:T(8,128)(2,1)S(1)}, bf16[2,16,4096]{2,1,0:T(8,128)(2,1)}, u32[]{:S(2)}) copy-start(bf16[2,16,4096]{2,1,0:T(8,128)(2,1)} %param.23) | copy-start | bytes 786436
  13.1 14.2 %copy-start.2 = (s32[1,32]{1,0:T(1,128)S(1)}, s32[1,32]{1,0:T(1,128)}, u32[]{:S(2)}) copy-start(s32[1,32]{1,0:T(1,128)} %param.29) | copy-start | bytes 388
  14.3 30.4 %all-to-all-start = ((bf16[8,4,16,512]{3,2,1,0:T(8,128)(2,1)}), bf16[8,4,16,512]{3,2,1,0:T(8,128)(2,1)S(1)}, u32[]{:S(2)}, u32[]{:S(2)}) async-start(bf16[8,4,16,512]{3,2,1,0:T(8,128)(2,1)} %param.27), calls=%async_computation | async-start | bytes 1048576 | tf_op jit(solution)/shard_map/all_to_all | solution.py:206
  19.4 213.2 %reduce-scatter.2.cloned.1.call-start = ((), (), s32[]{:S(2)}) async-start(), calls=%async_computation.3 | async-start | bytes 6782976 | tf_op jit(solution)/shard_map/reduce_scatter | solution.py:175
  19.7 22.5 %collective-permute-start.6 = (bf16[1,4,16,512]{3,2,1,0:T(8,128)(2,1)S(1)}, bf16[1,4,16,512]{3,2,1,0:T(8,128)(2,1)S(1)}, u32[]{:S(2)}, u32[]{:S(2)}) collective-permute-start(bf16[1,4,16,512]{3,2,1,0:T(8,128)(2,1)S(1)} %get-tuple-element.13), channel_id=1, source_target_pairs={{0,28},{4,24},{8,20},{12,16},{16,12},{20,8},{24,4},{28,0},{1,29},{... | collective-permute-start | bytes 196616 | tf_op jit(solution)/shard_map/ppermute | solution.py:30
  22.3 16.2 %collective-permute-start.4 = (bf16[1,4,16,512]{3,2,1,0:T(8,128)(2,1)S(1)}, bf16[1,4,16,512]{3,2,1,0:T(8,128)(2,1)S(1)}, u32[]{:S(2)}, u32[]{:S(2)}) collective-permute-start(bf16[1,4,16,512]{3,2,1,0:T(8,128)(2,1)S(1)} %get-tuple-element.14), channel_id=1, source_target_pairs={{0,20},{4,16},{8,28},{12,24},{16,4},{20,0},{24,12},{28,8},{1,21},{... | collective-permute-start | bytes 196616 | tf_op jit(solution)/shard_map/ppermute | solution.py:30
  22.8 15.6 %collective-permute-start.3 = (bf16[1,4,16,512]{3,2,1,0:T(8,128)(2,1)S(1)}, bf16[1,4,16,512]{3,2,1,0:T(8,128)(2,1)S(1)}, u32[]{:S(2)}, u32[]{:S(2)}) collective-permute-start(bf16[1,4,16,512]{3,2,1,0:T(8,128)(2,1)S(1)} %get-tuple-element.15), channel_id=1, source_target_pairs={{0,16},{4,20},{8,24},{12,28},{16,0},{20,4},{24,8},{28,12},{1,17},{... | collective-permute-start | bytes 196616 | tf_op jit(solution)/shard_map/ppermute | solution.py:30
  24.3 14.1 %collective-permute-start.2 = (bf16[1,4,16,512]{3,2,1,0:T(8,128)(2,1)S(1)}, bf16[1,4,16,512]{3,2,1,0:T(8,128)(2,1)S(1)}, u32[]{:S(2)}, u32[]{:S(2)}) collective-permute-start(bf16[1,4,16,512]{3,2,1,0:T(8,128)(2,1)S(1)} %get-tuple-element.16), channel_id=1, source_target_pairs={{0,12},{4,8},{8,4},{12,0},{16,28},{20,24},{24,20},{28,16},{1,13},{... | collective-permute-start | bytes 196616 | tf_op jit(solution)/shard_map/ppermute | solution.py:30
  24.4 8.3 %collective-permute-start = (bf16[1,4,16,512]{3,2,1,0:T(8,128)(2,1)S(1)}, bf16[1,4,16,512]{3,2,1,0:T(8,128)(2,1)S(1)}, u32[]{:S(2)}, u32[]{:S(2)}) collective-permute-start(bf16[1,4,16,512]{3,2,1,0:T(8,128)(2,1)S(1)} %get-tuple-element.18), channel_id=1, source_target_pairs={{0,4},{4,0},{8,12},{12,8},{16,20},{20,16},{24,28},{28,24},{1,5},{5... | collective-permute-start | bytes 196616 | tf_op jit(solution)/shard_map/ppermute | solution.py:30
  32.6 4.3 %collective-permute-start.1 = (bf16[1,4,16,512]{3,2,1,0:T(8,128)(2,1)S(1)}, bf16[1,4,16,512]{3,2,1,0:T(8,128)(2,1)S(1)}, u32[]{:S(2)}, u32[]{:S(2)}) collective-permute-start(bf16[1,4,16,512]{3,2,1,0:T(8,128)(2,1)S(1)} %get-tuple-element.17), channel_id=1, source_target_pairs={{0,8},{4,12},{8,0},{12,4},{16,24},{20,28},{24,16},{28,20},{1,9},{5... | collective-permute-start | bytes 196616 | tf_op jit(solution)/shard_map/ppermute | solution.py:30
  37.0 5.2 %collective-permute-start.5 = (bf16[1,4,16,512]{3,2,1,0:T(8,128)(2,1)S(1)}, bf16[1,4,16,512]{3,2,1,0:T(8,128)(2,1)S(1)}, u32[]{:S(2)}, u32[]{:S(2)}) collective-permute-start(bf16[1,4,16,512]{3,2,1,0:T(8,128)(2,1)S(1)} %get-tuple-element.20), channel_id=1, source_target_pairs={{0,24},{4,28},{8,16},{12,20},{16,8},{20,12},{24,0},{28,4},{1,25},{... | collective-permute-start | bytes 196616 | tf_op jit(solution)/shard_map/ppermute | solution.py:30
  63.2 8.2 %slice-start = ((s8[5242880]{0:T(1024)(128)(4,1)}), s8[4194304]{0:T(1024)(128)(4,1)S(1)}, s32[]{:S(2)}) async-start(s8[5242880]{0:T(1024)(128)(4,1)} %bitcast.96), calls=%async_computation.5 | async-start | bytes 8388608
  63.2 6.6 %copy-start.6 = (f32[2,16,8,8,2]{3,4,0,2,1:T(2,128)S(1)}, f32[2,16,8,8,2]{3,4,0,2,1:T(2,128)}, u32[]{:S(2)}) copy-start(f32[2,16,8,8,2]{3,4,0,2,1:T(2,128)} %get-tuple-element.28) | copy-start | bytes 49156
  63.2 8.2 %slice-start.1 = ((s8[5242880]{0:T(1024)(128)(4,1)}), s8[1048576]{0:T(1024)(128)(4,1)S(1)}, s32[]{:S(2)}) async-start(s8[5242880]{0:T(1024)(128)(4,1)} %bitcast.96), calls=%async_computation.6 | async-start | bytes 2097152
  71.4 1.5 copy-start.7
  173.2 83.5 %copy-start.3 = (bf16[2,16,2880]{2,1,0:T(8,128)(2,1)S(1)}, bf16[2,16,2880]{2,1,0:T(8,128)(2,1)}, u32[]{:S(2)}) copy-start(bf16[2,16,2880]{2,1,0:T(8,128)(2,1)} %param.16) | copy-start | bytes 552964
  173.2 84.2 %copy-start.1 = (bf16[2880,64]{0,1:T(8,128)(2,1)S(1)}, bf16[2880,64]{0,1:T(8,128)(2,1)}, u32[]{:S(2)}) copy-start(bf16[2880,64]{0,1:T(8,128)(2,1)} %param.18) | copy-start | bytes 1105924
Sparse Core Ops, SparseCore 0:
  14.4 73.6 all-gather.2
  173.3 59.2 reduce-scatter.1
